TPU v7x, 32 devices: a whole 2x2x4 slice. The times are simulated.
32 devices in a mesh: seq: 4 (over y, x), tp: 8 (over z, core).
Axes of the slice: x: 2, y: 2, z: 4, core: 2. Of those that a mesh axis runs over, the one named last changes fastest.
Arguments:
- streams: bfloat16 [3, 4096, 1024], P(None, 'tp', 'seq'), may hold values from -6 to 6
- feat_weight: float32 [3, 4096, 7], P(None, 'tp'), may hold values from -2 to 2
- long_filter: float32 [4096, 128], P('tp'), may hold values from -0.5 to 0.5
- skip_gain: float32 [4096], P('tp'), may hold values from -1 to 1
- out_weight: bfloat16 [4096, 4096], P('tp', 'seq'), may hold values from -0.125 to 0.125
- out_grad: bfloat16 [4096, 1024], P('tp', 'seq'), may hold values from -6 to 6
Outputs:
- mixed: bfloat16 [4096, 1024], P('tp', 'seq')
- stream_grad: bfloat16 [3, 4096, 1024], P(None, 'tp', 'seq')
- weight_grad: bfloat16 [4096, 4096], P('tp', 'seq')
All inputs are finite; a program needn't handle non-finite values.
Results may differ from a plain program's by a relative error of at most 0.009.
Values may be sent and summed in bfloat16 or wider, within the bound.
No kernel may reach another device: no remote copies, remote signals or barrier semaphores. Data moves between devices by JAX's collectives and lax.ppermute only.
A program may use at most 64 MiB of HBM per device.

v0:
```python
import math
import jax
import jax.numpy as jnp
from jax import lax
from jax.sharding import PartitionSpec as P


def extended(block, sides, width):
    for axis, dim in sides:
        count = lax.axis_size(axis)
        forward = [(i, i + 1) for i in range(count - 1)]
        backward = [(target, source) for source, target in forward]
        low = lax.ppermute(
            lax.slice_in_dim(block, block.shape[dim] - width, None, axis=dim), axis, forward
        )
        high = lax.ppermute(lax.slice_in_dim(block, 0, width, axis=dim), axis, backward)
        block = jnp.concatenate([low, block, high], axis=dim)
    return block


def from_behind(block, axis, distance):
    devices = range(lax.axis_size(axis))
    route = [(i - distance, i) for i in devices if i - distance in devices]
    return lax.ppermute(block, axis, route)


def correlate(signal, taps):
    return lax.conv_general_dilated(
        signal[None],
        taps[:, None, :],
        (1,),
        "VALID",
        dimension_numbers=("NCH", "OIH", "NCH"),
        feature_group_count=signal.shape[0],
        precision=lax.Precision.HIGHEST,
    )[0]


def rows_of_slab(out_grad, n_seq, n_tp):
    rows, length = out_grad.shape
    piece = rows // n_seq
    split = out_grad.reshape(n_seq, piece, length)
    mine = lax.all_to_all(split, "seq", 0, 0)
    mine = jnp.transpose(mine, (1, 0, 2)).reshape(piece, n_seq * length)
    route = []
    for a in range(n_seq):
        for b in range(n_tp):
            flat = n_seq * b + a
            route.append((a * n_tp + b, flat // n_tp * n_tp + flat % n_tp))
    moved = lax.ppermute(mine, ("seq", "tp"), route)
    return lax.all_gather(moved, "tp", axis=0, tiled=True)


def shards(streams, feat_weight, long_filter, skip_gain, out_weight, out_grad):
    channels = streams.shape[1]
    length = streams.shape[2]
    taps_long = long_filter.shape[1]
    taps_short = feat_weight.shape[2]
    n_seq = lax.axis_size("seq")
    n_tp = lax.axis_size("tp")
    reach = taps_long + taps_short - 2
    slab_grad = rows_of_slab(out_grad, n_seq, n_tp)
    slab_width = slab_grad.shape[0]
    partial_grad = jnp.dot(out_weight, slab_grad, preferred_element_type=jnp.float32)
    gated_grad = lax.psum_scatter(partial_grad, "seq", scatter_dimension=1, tiled=True)
    widened = extended(streams, (("seq", 2),), reach).astype(jnp.float32)
    short_taps = feat_weight.reshape(3 * channels, taps_short)
    feats = correlate(
        widened.reshape(3 * channels, length + 2 * reach), short_taps[:, ::-1]
    ).reshape(3, channels, -1)
    query_feat, key_feat, value_feat = (feats[0], feats[1], feats[2])
    product = key_feat * value_feat
    convolved = correlate(product, long_filter[:, ::-1])
    summed = convolved + skip_gain[:, None] * product[:, taps_long - 1 :]
    query_tail = query_feat[:, taps_long - 1 :]
    gated = (query_tail[:, :length] * summed[:, :length]).astype(jnp.bfloat16)
    gated_all = lax.all_gather(gated, "seq", axis=1, tiled=True)
    partial_out = lax.dot_general(
        out_weight, gated_all, (((0,), (0,)), ((), ())), preferred_element_type=jnp.float32
    )
    group = n_tp // n_seq
    out_rows = slab_width // group
    partial_out = (
        partial_out.reshape(group, out_rows, n_seq, length)
        .transpose(0, 2, 1, 3)
        .reshape(n_tp * out_rows, length)
    )
    output_sum = lax.psum_scatter(partial_out, "tp", scatter_dimension=0, tiled=True)
    route = []
    for s in range(n_seq):
        for p in range(n_tp):
            route.append((s * n_tp + p, p % n_seq * n_tp + group * s + p // n_seq))
    mixed = lax.ppermute(output_sum.astype(jnp.bfloat16), ("seq", "tp"), route)
    scale = 1.0 / math.sqrt(length * n_seq)
    terms = lax.dot_general(
        gated_all.reshape(channels, n_seq, length),
        slab_grad.reshape(slab_width, n_seq, length),
        (((2,), (2,)), ((1,), (1,))),
        preferred_element_type=jnp.float32,
    )
    terms = lax.reduce_precision(terms * scale, exponent_bits=8, mantissa_bits=7)
    weight_grad = jnp.sum(terms, axis=0).astype(jnp.bfloat16)
    next_grad = from_behind(gated_grad[:, :reach].astype(jnp.bfloat16), "seq", -1).astype(
        jnp.float32
    )
    grad_ext = jnp.concatenate([gated_grad, next_grad], axis=1)
    conv_grad = grad_ext * query_tail
    keep = length + taps_short - 1
    prod_grad = correlate(conv_grad, long_filter) + skip_gain[:, None] * conv_grad[:, :keep]
    query_grad = grad_ext[:, :keep] * summed[:, :keep]
    key_grad = prod_grad * value_feat[:, taps_long - 1 : taps_long - 1 + keep]
    value_grad = prod_grad * key_feat[:, taps_long - 1 : taps_long - 1 + keep]
    feat_grad = jnp.stack([query_grad, key_grad, value_grad]).reshape(3 * channels, keep)
    stream_grad = correlate(feat_grad, short_taps).reshape(3, channels, length).astype(jnp.bfloat16)
    return (mixed, stream_grad, weight_grad)


def solution(mesh):
    return jax.shard_map(
        shards,
        mesh=mesh,
        in_specs=(
            P(None, "tp", "seq"),
            P(None, "tp", None),
            P("tp", None),
            P("tp"),
            P("tp", "seq"),
            P("tp", "seq"),
        ),
        out_specs=(P("tp", "seq"), P(None, "tp", "seq"), P("tp", "seq")),
        check_vma=False,
    )
```

profile of v0, /device:TPU:4, one launch (start us, length us, event | category | flops | bytes accessed | tf_op | source)
XLA Modules:
  0.0 241.9 jit_solution(13884115816914673931)
XLA Ops:
  7.2 4.4 %all-to-all-start = ((bf16[4,128,256]{2,1,0:T(8,128)(2,1)}), bf16[4,128,256]{2,1,0:T(8,128)(2,1)S(1)}, u32[]{:S(2)}, u32[]{:S(2)}) async-start(bf16[4,128,256]{2,1,0:T(8,128)(2,1)} %bitcast.78), calls=%async_computation.1 | async-start | bytes 524288 | tf_op jit(solution)/shard_map/all_to_all | solution.py:43
  11.5 1.8 fusion.35
  13.4 1.0 copy.89
  14.4 3.4 %collective-permute-start = (bf16[3,512,133]{1,2,0:T(8,128)(2,1)}, bf16[3,512,133]{1,2,0:T(8,128)(2,1)S(1)}, u32[]{:S(2)}, u32[]{:S(2)}) collective-permute-start(bf16[3,512,133]{1,2,0:T(8,128)(2,1)} %copy.89), channel_id=1, source_target_pairs={{0,8},{8,16},{16,24},{1,9},{9,17},{17,25},{2,10},{10,18},{18,26},{... | collective-permute-start | bytes 1225736 | tf_op jit(solution)/shard_map/ppermute | solution.py:13
  17.8 1.0 copy.90
  18.8 3.4 %collective-permute-start.1 = (bf16[3,512,133]{1,2,0:T(8,128)(2,1)}, bf16[3,512,133]{1,2,0:T(8,128)(2,1)S(1)}, u32[]{:S(2)}, u32[]{:S(2)}) collective-permute-start(bf16[3,512,133]{1,2,0:T(8,128)(2,1)} %copy.90), channel_id=1, source_target_pairs={{8,0},{16,8},{24,16},{9,1},{17,9},{25,17},{10,2},{18,10},{26,18},{... | collective-permute-start | bytes 1225736 | tf_op jit(solution)/shard_map/ppermute | solution.py:16
  22.3 1.9 collective-permute-start.3
  24.3 0.3 rev.6
  24.6 0.4 rev.7
  25.0 0.9 copy.68
  25.8 7.5 %collective-permute-done = bf16[3,512,133]{1,2,0:T(8,128)(2,1)S(1)} collective-permute-done((bf16[3,512,133]{1,2,0:T(8,128)(2,1)}, bf16[3,512,133]{1,2,0:T(8,128)(2,1)S(1)}, u32[]{:S(2)}, u32[]{:S(2)}) %collective-permute-start) | collective-permute-done | bytes 408608 | tf_op jit(solution)/shard_map/ppermute | solution.py:13
  33.4 1.2 copy.60
  34.5 0.8 collective-permute-done.1
  35.4 1.2 copy.61
  36.5 0.7 copy-done.12
  37.5 2.6 %pad_maximum_fusion = bf16[3,512,522]{2,1,0:T(8,128)(2,1)S(1)} fusion(bf16[3,512,133]{2,1,0:T(8,128)(2,1)} %copy.61, bf16[3,512,256]{2,1,0:T(8,128)(2,1)} %param.6, bf16[3,512,133]{2,1,0:T(8,128)(2,1)} %copy.60), kind=kLoop, calls=%fused_computation.7 | loop fusion | flops 4810752 | bytes 3207168 | tf_op jit(solution)/shard_map/concatenate | solution.py:17
  40.0 2.2 copy.62
  42.3 2.7 %pad = bf16[1536,1,528]{0,2,1:T(8,128)(2,1)} pad(bf16[1536,1,522]{0,2,1:T(8,128)(2,1)} %copy.62, bf16[]{:T(256)} %constant.12), padding=0_0x0_0x0_6 | pad | bytes 3225602 | tf_op jit(solution)/shard_map/broadcast_in_dim;reshape | solution.py:29
  45.0 1.6 reshape.44
  46.6 0.5 copy.64
  47.3 1.7 convolution_select_fusion
  49.0 1.7 fusion.34
  50.7 0.6 copy.69
  51.4 1.1 reshape.50
  52.5 1.9 copy.70
  54.4 1.1 reshape.52
  55.5 1.9 copy.65
  57.4 1.1 reshape.48
  58.5 0.6 copy.66
  59.2 2.3 reshape.75
  61.5 1.2 copy-done.7
  62.7 1.9 slice_bitcast_fusion
  64.7 21.2 %fusion.36 = f32[1,512,389]{1,0,2:T(1,128)S(1)} fusion(f32[1,528,512]{2,0,1:T(1,128)S(1)} %copy-done.9, f32[512,1,128]{0,1,2:T(1,128)S(1)} %copy-done.13), kind=kOutput, calls=%fused_computation.57 | convolution fusion | flops 305922048 | bytes 2140160 | tf_op jit(solution)/shard_map/conv_general_dilated | solution.py:28
  85.9 0.3 fusion.17
  86.2 0.9 copy-done.4
  87.1 0.8 fusion.26
  88.0 4.2 %fusion.37 = f32[512,1024]{0,1:T(8,128)} fusion(bf16[512,1024]{1,0:T(8,128)(2,1)S(1)} %copy-done, bf16[1024,1024]{0,1:T(8,128)(2,1)} %all-gather.5.cloned.1.call-done), kind=kOutput, calls=%fused_computation.58 | convolution fusion | flops 1073741824 | bytes 5242880 | tf_op jit(solution)/shard_map/dot_general | solution.py:64
  92.3 0.3 reduce-scatter.3.cloned.1.call-start
  92.6 29.9 %all-gather.3.cloned.1.call-done = bf16[512,1024]{0,1:T(8,128)(2,1)} async-done(((bf16[512,256]{0,1:T(8,128)(2,1)}), bf16[512,1024]{0,1:T(8,128)(2,1)}) %all-gather.3.cloned.1.call-update) | async-done | bytes 1048592 | tf_op jit(solution)/shard_map/all_gather | solution.py:77
  122.5 4.4 %convolution_bitcast_fusion = f32[1024,1024]{0,1:T(8,128)} fusion(bf16[512,1024]{0,1:T(8,128)(2,1)} %all-gather.3.cloned.1.call-done, bf16[512,1024]{1,0:T(8,128)(2,1)S(1)} %copy-done), kind=kOutput, calls=%fused_computation.6 | convolution fusion | flops 1073741824 | bytes 6291456 | tf_op jit(solution)/shard_map/dot_general | solution.py:78
  126.9 6.7 %reshape.36 = f32[2,512,4,256]{1,0,3,2:T(2,128)} reshape(f32[1024,1024]{0,1:T(8,128)} %convolution_bitcast_fusion) | data formatting | bytes 8388608 | tf_op jit(solution)/shard_map/reshape | solution.py:84
  133.6 7.3 %copy.71 = f32[2,4,512,256]{3,2,1,0:T(8,128)} copy(f32[2,4,512,256]{2,0,3,1:T(2,128)} %bitcast.71) | data formatting | bytes 8388608 | tf_op jit(solution)/shard_map/transpose | solution.py:85
  140.9 0.9 copy-done.11
  142.0 18.7 %reduce-scatter.5.cloned.1.call-done = f32[512,256]{0,1:T(8,128)} async-done(((f32[512,1024]{0,1:T(8,128)}), f32[512,256]{0,1:T(8,128)}) %reduce-scatter.5.cloned.1.call-update) | async-done | bytes 524304 | tf_op jit(solution)/shard_map/reduce_scatter | solution.py:65
  160.7 1.0 slice.138
  161.6 3.4 %collective-permute-start.4 = (bf16[512,133]{0,1:T(8,128)(2,1)S(1)}, bf16[512,133]{0,1:T(8,128)(2,1)S(1)}, u32[]{:S(2)}, u32[]{:S(2)}) collective-permute-start(bf16[512,133]{0,1:T(8,128)(2,1)S(1)} %slice.138), channel_id=1, source_target_pairs={{8,0},{16,8},{24,16},{9,1},{17,9},{25,17},{10,2},{18,10},{26,18},{... | collective-permute-start | bytes 408584 | tf_op jit(solution)/shard_map/ppermute | solution.py:24
  165.0 4.7 %reduce-precision_reduce_fusion = bf16[512,1024]{1,0:T(8,128)(2,1)} fusion(bf16[512,4,256]{0,2,1:T(8,128)(2,1)} %bitcast.83, bf16[1024,4,256]{0,2,1:T(8,128)(2,1)} %bitcast.82), kind=kOutput, calls=%fused_computation | convolution fusion | flops 1079508992 | bytes 4194304 | tf_op jit(solution)/shard_map/dot_general | solution.py:95
  169.9 1.1 copy-done.3
  171.1 5.4 %fusion.18 = f32[1,512,262]{1,0,2:T(1,128)S(1)} fusion(f32[512,1,128]{0,1,2:T(1,128)S(1)} %copy.75, f32[1,512,389]{1,2,0:T(8,128)S(1)} %bitcast.73), kind=kOutput, calls=%fused_computation.32 | convolution fusion | flops 206045184 | bytes 1595392 | tf_op jit(solution)/shard_map/conv_general_dilated | solution.py:28
  176.6 0.3 fusion.24
  177.0 1.1 copy.76
  178.1 2.4 reshape.69
  180.4 2.7 %pad.2 = f32[1536,1,264]{0,2,1:T(8,128)} pad(f32[1536,1,262]{0,2,1:T(8,128)} %reshape.69, f32[]{:T(128)} %constant.11.clone.1), padding=0_0x0_0x0_2 | pad | bytes 3231748 | tf_op jit(solution)/shard_map/broadcast_in_dim;reshape | solution.py:29
  183.2 3.2 %reshape.55 = f32[1536,1,8,33]{0,1,3,2:T(1,128)S(1)} reshape(f32[1536,1,264]{0,2,1:T(8,128)} %pad.2) | data formatting | bytes 3244032 | tf_op jit(solution)/shard_map/conv_general_dilated | solution.py:28
  186.6 0.5 copy-done.17
  187.1 1.5 fusion.1
  188.6 0.3 copy.80
  188.9 0.3 reshape.59
  189.2 23.6 %reduce-scatter.3.cloned.1.call-done = f32[512,256]{1,0:T(8,128)} async-done(((f32[4096,256]{1,0:T(8,128)}), f32[512,256]{1,0:T(8,128)}) %reduce-scatter.3.cloned.1.call-update) | async-done | bytes 524304 | tf_op jit(solution)/shard_map/reduce_scatter | solution.py:88
  212.8 1.2 convert_element_type.21
  213.9 1.9 collective-permute-start.2
  215.9 1.2 copy.81
  217.1 17.6 %collective-permute-done.2 = bf16[512,256]{1,0:T(8,128)(2,1)S(1)} collective-permute-done((bf16[512,256]{1,0:T(8,128)(2,1)S(1)}, bf16[512,256]{1,0:T(8,128)(2,1)S(1)}, u32[]{:S(2)}, u32[]{:S(2)}) %collective-permute-start.2) | collective-permute-done | bytes 262176 | tf_op jit(solution)/shard_map/ppermute | solution.py:93
  234.7 0.7 copy.102
  (53 shorter events, 1.8 us)
Async XLA Ops:
  7.2 80.8 %copy-start = (bf16[512,1024]{1,0:T(8,128)(2,1)S(1)}, bf16[512,1024]{1,0:T(8,128)(2,1)}, u32[]{:S(2)}) copy-start(bf16[512,1024]{1,0:T(8,128)(2,1)} %param.10) | copy-start | bytes 3145732
  7.2 15.0 %all-to-all-start = ((bf16[4,128,256]{2,1,0:T(8,128)(2,1)}), bf16[4,128,256]{2,1,0:T(8,128)(2,1)S(1)}, u32[]{:S(2)}, u32[]{:S(2)}) async-start(bf16[4,128,256]{2,1,0:T(8,128)(2,1)} %bitcast.78), calls=%async_computation.1 | async-start | bytes 524288 | tf_op jit(solution)/shard_map/all_to_all | solution.py:43
  11.5 76.5 %all-gather.5.cloned.1.call-start = ((), (), s32[]{:S(2)}) async-start(), calls=%async_computation.5 | async-start | bytes 2359296 | tf_op jit(solution)/shard_map/all_gather | solution.py:51
  13.4 10.9 %copy-start.14 = (f32[3,512,7]{1,2,0:T(8,128)S(1)}, f32[3,512,7]{1,2,0:T(8,128)}, u32[]{:S(2)}) copy-start(f32[3,512,7]{1,2,0:T(8,128)} %param.7) | copy-start | bytes 129028
  13.4 11.2 %copy-start.10 = (f32[512,128]{1,0:T(8,128)S(1)}, f32[512,128]{1,0:T(8,128)}, u32[]{:S(2)}) copy-start(f32[512,128]{1,0:T(8,128)} %param.8) | copy-start | bytes 786436
  14.4 19.0 %collective-permute-start = (bf16[3,512,133]{1,2,0:T(8,128)(2,1)}, bf16[3,512,133]{1,2,0:T(8,128)(2,1)S(1)}, u32[]{:S(2)}, u32[]{:S(2)}) collective-permute-start(bf16[3,512,133]{1,2,0:T(8,128)(2,1)} %copy.89), channel_id=1, source_target_pairs={{0,8},{8,16},{16,24},{1,9},{9,17},{17,25},{2,10},{10,18},{18,26},{... | collective-permute-start | bytes 1225736 | tf_op jit(solution)/shard_map/ppermute | solution.py:13
  18.8 16.6 %collective-permute-start.1 = (bf16[3,512,133]{1,2,0:T(8,128)(2,1)}, bf16[3,512,133]{1,2,0:T(8,128)(2,1)S(1)}, u32[]{:S(2)}, u32[]{:S(2)}) collective-permute-start(bf16[3,512,133]{1,2,0:T(8,128)(2,1)} %copy.90), channel_id=1, source_target_pairs={{8,0},{16,8},{24,16},{9,1},{17,9},{25,17},{10,2},{18,10},{26,18},{... | collective-permute-start | bytes 1225736 | tf_op jit(solution)/shard_map/ppermute | solution.py:16
  22.3 14.2 %collective-permute-start.3 = (bf16[128,1024]{0,1:T(8,128)(2,1)S(1)}, bf16[128,1024]{0,1:T(8,128)(2,1)S(1)}, u32[]{:S(2)}, u32[]{:S(2)}) collective-permute-start(bf16[128,1024]{0,1:T(8,128)(2,1)S(1)} %bitcast.79), channel_id=1, source_target_pairs={{0,0},{1,4},{2,8},{3,12},{4,16},{5,20},{6,24},{7,28},{8,1},{9,5},{... | collective-permute-start | bytes 786440 | tf_op jit(solution)/shard_map/ppermute | solution.py:50
  36.5 0.7 copy-start.12
  37.3 85.2 %all-gather.3.cloned.1.call-start = ((), (), s32[]{:S(2)}) async-start(), calls=%async_computation.3 | async-start | bytes 1310720 | tf_op jit(solution)/shard_map/all_gather | solution.py:77
  46.6 0.7 copy-start.16
  59.2 2.3 copy-start.6
  61.5 1.2 copy-start.7
  62.7 23.5 %copy-start.2 = (f32[512,516]{0,1:T(8,128)}, f32[512,516]{0,1:T(8,128)S(1)}, u32[]{:S(2)}) copy-start(f32[512,516]{0,1:T(8,128)S(1)} %slice_bitcast_fusion.2) | copy-start | bytes 3170308
  62.7 2.0 copy-start.9
  62.7 2.0 copy-start.13
  64.7 21.2 %copy-start.15 = (f32[512]{0:T(512)S(1)}, f32[512]{0:T(512)}, u32[]{:S(2)}) copy-start(f32[512]{0:T(512)} %param.9) | copy-start | bytes 6148
  86.2 0.9 copy-start.4
  87.9 72.7 %reduce-scatter.5.cloned.1.call-start = ((), (), s32[]{:S(2)}) async-start(), calls=%async_computation.6 | async-start | bytes 2621440 | tf_op jit(solution)/shard_map/reduce_scatter | solution.py:65
  92.3 120.5 %reduce-scatter.3.cloned.1.call-start = ((), (), s32[]{:S(2)}) async-start(), calls=%async_computation.4 | async-start | bytes 4718592 | tf_op jit(solution)/shard_map/reduce_scatter | solution.py:88
  140.8 1.0 copy-start.11
  161.6 8.1 %collective-permute-start.4 = (bf16[512,133]{0,1:T(8,128)(2,1)S(1)}, bf16[512,133]{0,1:T(8,128)(2,1)S(1)}, u32[]{:S(2)}, u32[]{:S(2)}) collective-permute-start(bf16[512,133]{0,1:T(8,128)(2,1)S(1)} %slice.138), channel_id=1, source_target_pairs={{8,0},{16,8},{24,16},{9,1},{17,9},{25,17},{10,2},{18,10},{26,18},{... | collective-permute-start | bytes 408584 | tf_op jit(solution)/shard_map/ppermute | solution.py:24
  165.0 4.7 %copy-start.5 = (f32[512,389]{0,1:T(8,128)S(1)}, f32[512,389]{0,1:T(8,128)}, u32[]{:S(2)}) copy-start(f32[512,389]{0,1:T(8,128)} %copy-done.4) | copy-start | bytes 2390020
  165.0 4.7 %copy-start.8 = (f32[512,256]{0,1:T(8,128)S(1)}, f32[512,256]{0,1:T(8,128)}, u32[]{:S(2)}) copy-start(f32[512,256]{0,1:T(8,128)} %reduce-scatter.5.cloned.1.call-done) | copy-start | bytes 1572868
  169.7 1.2 copy-start.3
  186.4 0.7 copy-start.17
  212.8 22.6 %copy-start.1 = (bf16[512,1024]{1,0:T(8,128)(2,1)S(1)}, bf16[512,1024]{1,0:T(8,128)(2,1)}, u32[]{:S(2)}) copy-start(bf16[512,1024]{1,0:T(8,128)(2,1)} %param.10) | copy-start | bytes 3145732
  213.9 20.7 %collective-permute-start.2 = (bf16[512,256]{1,0:T(8,128)(2,1)S(1)}, bf16[512,256]{1,0:T(8,128)(2,1)S(1)}, u32[]{:S(2)}, u32[]{:S(2)}) collective-permute-start(bf16[512,256]{1,0:T(8,128)(2,1)S(1)} %convert_element_type.21), channel_id=1, source_target_pairs={{0,0},{1,8},{2,16},{3,24},{4,1},{5,9},{6,17},{7,25},{8,2},{9,10},{... | collective-permute-start | bytes 786440 | tf_op jit(solution)/shard_map/ppermute | solution.py:93
Sparse Core Ops, SparseCore 0:
  37.4 38.2 all-gather.4
  88.1 34.3 all-gather.2
  125.4 35.1 reduce-scatter.4
  162.8 49.9 reduce-scatter.2
where the time goes:
time: 243 us; the launch traced here: 242 us
  waiting for transfers between devices  98.2 us (40%)
  local copies, waits for them, and re-layouts  60.3 us (25%)
  matrix products  43.1 us (18%)
  starting transfers between devices  18.8 us (8%)
  between operations  14.2 us (6%)
  other arithmetic  7.25 us (3%)
    all_gather x1, waiting for transfers between devices, shards(): gated_all = lax.all_gather(gated, 'seq', axis=1, tiled=True)  29.9 us
    conv_general_dilated x4, matrix products, correlate(): lax.conv_general_dilated(signal[None], taps[:, None, :], (1,), 'VALID', d...  29.8 us
    reduce_scatter x1, waiting for transfers between devices, shards(): lax.psum_scatter(partial_out, 'tp', scatter_dimension=0, tiled=True)  23.6 us
    reduce_scatter x1, waiting for transfers between devices, shards(): lax.psum_scatter(partial_grad, 'seq', scatter_dimension=1, tiled=True)  18.7 us
    ppermute x1, waiting for transfers between devices, shards(): mixed = lax.ppermute(output_sum.astype(jnp.bfloat16), ('seq', 'tp'), route)  17.6 us
    conv_general_dilated x12, local copies, waits for them, and re-layouts, correlate(): lax.conv_general_dilated(signal[None], taps[:, None, :], (1,), 'VALID', d...  13.3 us
    another operation x4, local copies, waits for them, and re-layouts, correlate(): signal[None]  9.99 us
    unnamed x39, local copies, waits for them, and re-layouts  8.37 us
  transfers between devices with their start and end apart: 10, of which 6 were waited for; matrix products, arithmetic and copies ran while one was open for 43% of the time, Pallas kernels for 0%

commit v1 on v0

--- a/solution.py
+++ b/solution.py
@@ -3,6 +3,14 @@
 import jax.numpy as jnp
 from jax import lax
 from jax.sharding import PartitionSpec as P
+
+
+def gather_from_all(value, axis, dim):
+    size = lax.axis_size(axis)
+    repeats = [size if d == dim else 1 for d in range(value.ndim)]
+    return lax.all_to_all(
+        jnp.tile(value, repeats), axis, split_axis=dim, concat_axis=dim, tiled=True
+    )
 
 
 def extended(block, sides, width):
@@ -74,7 +82,7 @@
     summed = convolved + skip_gain[:, None] * product[:, taps_long - 1 :]
     query_tail = query_feat[:, taps_long - 1 :]
     gated = (query_tail[:, :length] * summed[:, :length]).astype(jnp.bfloat16)
-    gated_all = lax.all_gather(gated, "seq", axis=1, tiled=True)
+    gated_all = gather_from_all(gated, "seq", 1)
     partial_out = lax.dot_general(
         out_weight, gated_all, (((0,), (0,)), ((), ())), preferred_element_type=jnp.float32
     )

time: 243 us -> 231 us (0.951)
  waiting for transfers between devices: 98.2 us -> 55.8 us
  blocking collectives: 0 us -> 28 us
  local copies, waits for them, and re-layouts: 60.3 us -> 63.9 us
    all_gather x1 -> x0, waiting for transfers between devices: 29.9 us -> none  [shards(): gated_all = lax.all_gather(gated, 'seq', axis=1, tiled=True)]
    all_to_all x0 -> x2, blocking collectives: none -> 28 us  [the longest x1 19 us: gather_from_all(): lax.all_to_all(jnp.tile(value, repeats), axis, split_axis=dim, concat_axi...]
    reduce_scatter x1, waiting for transfers between devices: 18.7 us -> 0.02 us  [shards(): lax.psum_scatter(partial_grad, 'seq', scatter_dimension=1, tiled=True)]
    ppermute x1, waiting for transfers between devices: 0.01 us -> 8.07 us  [rows_of_slab(): moved = lax.ppermute(mine, ('seq', 'tp'), route)]
    all_to_all x1 -> x0, starting transfers between devices: 4.36 us -> none  [rows_of_slab(): mine = lax.all_to_all(split, 'seq', 0, 0)]
    reduce_scatter x1, waiting for transfers between devices: 23.6 us -> 19.7 us  [shards(): lax.psum_scatter(partial_out, 'tp', scatter_dimension=0, tiled=True)]
    ppermute x1, waiting for transfers between devices: 0.83 us -> 3.41 us  [extended(): lax.ppermute(lax.slice_in_dim(block, 0, width, axis=dim), axis, backward)]
    unnamed x39 -> x45, local copies, waits for them, and re-layouts: 8.37 us -> 9.8 us
  transfers between devices with their start and end apart: 10 -> 8, of which waited for: 6 -> 5; matrix products, arithmetic and copies ran while one was open for 43% -> 44% of each run, Pallas kernels for 0% -> 0%
where the time goes in v1:
time: 231 us; the launch traced here: 230 us
  local copies, waits for them, and re-layouts  63.9 us (28%)
  waiting for transfers between devices  55.8 us (24%)
  matrix products  43.1 us (19%)
  blocking collectives  28 us (12%)
  starting transfers between devices  17.8 us (8%)
  between operations  14.2 us (6%)
  other arithmetic  7.23 us (3%)
    conv_general_dilated x4, matrix products, correlate(): lax.conv_general_dilated(signal[None], taps[:, None, :], (1,), 'VALID', d...  29.8 us
    reduce_scatter x1, waiting for transfers between devices, shards(): lax.psum_scatter(partial_out, 'tp', scatter_dimension=0, tiled=True)  19.7 us
    all_to_all x1, blocking collectives, gather_from_all(): lax.all_to_all(jnp.tile(value, repeats), axis, split_axis=dim, concat_axi...  19 us
    ppermute x1, waiting for transfers between devices, shards(): mixed = lax.ppermute(output_sum.astype(jnp.bfloat16), ('seq', 'tp'), route)  17.6 us
    conv_general_dilated x12, local copies, waits for them, and re-layouts, correlate(): lax.conv_general_dilated(signal[None], taps[:, None, :], (1,), 'VALID', d...  13.3 us
    another operation x4, local copies, waits for them, and re-layouts, correlate(): signal[None]  10.1 us
    unnamed x45, local copies, waits for them, and re-layouts  9.8 us
    all_to_all x1, blocking collectives, rows_of_slab(): mine = lax.all_to_all(split, 'seq', 0, 0)  8.98 us
  transfers between devices with their start and end apart: 8, of which 5 were waited for; matrix products, arithmetic and copies ran while one was open for 44% of the time, Pallas kernels for 0%

profile of v1, /device:TPU:4, one launch (start us, length us, event | category | flops | bytes accessed | tf_op | source)
XLA Modules:
  0.0 229.9 jit_solution(6504052412188928454)
XLA Ops:
  7.2 9.0 %all_to_all.14 = bf16[4,128,256]{2,1,0:T(8,128)(2,1)S(1)} all-to-all(bf16[4,128,256]{2,1,0:T(8,128)(2,1)} %bitcast.79), channel_id=1, replica_groups=mesh['seq'=4,'tp'=8] {'seq'}, dimensions={0} | all-to-all | bytes 524288 | tf_op jit(solution)/shard_map/all_to_all | solution.py:51
  16.4 4.0 %collective-permute-start.3 = (bf16[128,1024]{0,1:T(8,128)(2,1)S(1)}, bf16[128,1024]{0,1:T(8,128)(2,1)S(1)}, u32[]{:S(2)}, u32[]{:S(2)}) collective-permute-start(bf16[128,1024]{0,1:T(8,128)(2,1)S(1)} %bitcast.80), channel_id=1, source_target_pairs={{0,0},{1,4},{2,8},{3,12},{4,16},{5,20},{6,24},{7,28},{8,1},{9,5},{... | collective-permute-start | bytes 786440 | tf_op jit(solution)/shard_map/ppermute | solution.py:58
  20.4 8.1 %collective-permute-done.3 = bf16[128,1024]{0,1:T(8,128)(2,1)S(1)} collective-permute-done((bf16[128,1024]{0,1:T(8,128)(2,1)S(1)}, bf16[128,1024]{0,1:T(8,128)(2,1)S(1)}, u32[]{:S(2)}, u32[]{:S(2)}) %collective-permute-start.3) | collective-permute-done | bytes 262176 | tf_op jit(solution)/shard_map/ppermute | solution.py:58
  28.5 0.7 copy-done.16
  29.3 0.4 fusion.35
  29.7 1.0 copy.91
  30.7 4.7 %collective-permute-start = (bf16[3,512,133]{1,2,0:T(8,128)(2,1)}, bf16[3,512,133]{1,2,0:T(8,128)(2,1)S(1)}, u32[]{:S(2)}, u32[]{:S(2)}) collective-permute-start(bf16[3,512,133]{1,2,0:T(8,128)(2,1)} %copy.91), channel_id=1, source_target_pairs={{0,8},{8,16},{16,24},{1,9},{9,17},{17,25},{2,10},{10,18},{18,26},{... | collective-permute-start | bytes 1225736 | tf_op jit(solution)/shard_map/ppermute | solution.py:21
  35.6 3.3 %collective-permute-start.1 = (bf16[3,512,133]{1,2,0:T(8,128)(2,1)S(1)}, bf16[3,512,133]{1,2,0:T(8,128)(2,1)S(1)}, u32[]{:S(2)}, u32[]{:S(2)}) collective-permute-start(bf16[3,512,133]{1,2,0:T(8,128)(2,1)S(1)} %copy.92), channel_id=1, source_target_pairs={{8,0},{16,8},{24,16},{9,1},{17,9},{25,17},{10,2},{18,10},{26,18},{... | collective-permute-start | bytes 1225736 | tf_op jit(solution)/shard_map/ppermute | solution.py:24
  38.9 0.3 rev.6
  39.3 0.4 rev.7
  39.6 0.9 copy.70
  40.5 6.9 %collective-permute-done = bf16[3,512,133]{1,2,0:T(8,128)(2,1)S(1)} collective-permute-done((bf16[3,512,133]{1,2,0:T(8,128)(2,1)}, bf16[3,512,133]{1,2,0:T(8,128)(2,1)S(1)}, u32[]{:S(2)}, u32[]{:S(2)}) %collective-permute-start) | collective-permute-done | bytes 408608 | tf_op jit(solution)/shard_map/ppermute | solution.py:21
  47.4 1.2 copy.62
  48.6 3.4 %collective-permute-done.1 = bf16[3,512,133]{1,2,0:T(8,128)(2,1)S(1)} collective-permute-done((bf16[3,512,133]{1,2,0:T(8,128)(2,1)S(1)}, bf16[3,512,133]{1,2,0:T(8,128)(2,1)S(1)}, u32[]{:S(2)}, u32[]{:S(2)}) %collective-permute-start.1) | collective-permute-done | bytes 408608 | tf_op jit(solution)/shard_map/ppermute | solution.py:24
  52.0 1.2 copy.63
  53.1 2.5 %pad_maximum_fusion = bf16[3,512,522]{2,1,0:T(8,128)(2,1)S(1)} fusion(bf16[3,512,133]{2,1,0:T(8,128)(2,1)} %copy.63, bf16[3,512,256]{2,1,0:T(8,128)(2,1)} %param.6, bf16[3,512,133]{2,1,0:T(8,128)(2,1)} %copy.62), kind=kLoop, calls=%fused_computation.7 | loop fusion | flops 4810752 | bytes 3207168 | tf_op jit(solution)/shard_map/concatenate | solution.py:25
  55.7 2.3 %copy.64 = bf16[1536,1,522]{0,2,1:T(8,128)(2,1)} copy(bf16[1536,1,522]{2,0,1:T(8,128)(2,1)S(1)} %bitcast.72) | data formatting | bytes 3207168 | tf_op jit(solution)/shard_map/broadcast_in_dim;reshape | solution.py:37
  58.0 2.7 %pad = bf16[1536,1,528]{0,2,1:T(8,128)(2,1)} pad(bf16[1536,1,522]{0,2,1:T(8,128)(2,1)} %copy.64, bf16[]{:T(256)} %constant.12), padding=0_0x0_0x0_6 | pad | bytes 3225602 | tf_op jit(solution)/shard_map/broadcast_in_dim;reshape | solution.py:37
  60.7 1.7 reshape.49
  62.4 0.5 copy.66
  62.9 1.2 copy-done.10
  64.1 4.2 %fusion.37 = f32[512,1024]{0,1:T(8,128)} fusion(bf16[512,1024]{1,0:T(8,128)(2,1)S(1)} %copy-done, bf16[1024,1024]{0,1:T(8,128)(2,1)} %all-gather.2.cloned.1.call-done), kind=kOutput, calls=%fused_computation.58 | convolution fusion | flops 1073741824 | bytes 5242880 | tf_op jit(solution)/shard_map/dot_general | solution.py:72
  68.6 1.2 copy-done.11
  69.8 1.7 convolution_select_fusion
  71.5 1.7 fusion.34
  73.2 0.6 copy.71
  73.9 1.1 reshape.55
  75.0 1.9 copy.72
  76.8 1.1 reshape.57
  78.0 1.9 copy.67
  79.8 1.1 reshape.53
  81.0 0.6 copy.68
  81.6 2.3 reshape.80
  84.0 1.2 copy-done.8
  85.2 2.0 slice_bitcast_fusion
  87.3 21.1 %fusion.36 = f32[1,512,389]{1,0,2:T(1,128)S(1)} fusion(f32[1,528,512]{2,0,1:T(1,128)S(1)} %copy-done.12, f32[512,1,128]{0,1,2:T(1,128)S(1)} %copy-done.15), kind=kOutput, calls=%fused_computation.57 | convolution fusion | flops 305922048 | bytes 2140160 | tf_op jit(solution)/shard_map/conv_general_dilated | solution.py:36
  108.4 0.3 fusion.17
  108.7 0.9 copy-done.5
  109.6 0.8 fusion.26
  110.4 1.1 copy.73
  111.6 19.0 %all_to_all.15 = bf16[512,4,256]{2,0,1:T(8,128)(2,1)} all-to-all(bf16[512,4,256]{2,0,1:T(8,128)(2,1)S(1)} %tile.2), channel_id=1, replica_groups=mesh['seq'=4,'tp'=8] {'seq'}, dimensions={1} | all-to-all | bytes 2097152 | tf_op jit(solution)/shard_map/all_to_all | solution.py:11
  130.6 2.3 copy.74
  132.9 4.4 %convolution_bitcast_fusion = f32[1024,1024]{0,1:T(8,128)} fusion(bf16[512,1024]{0,1:T(8,128)(2,1)} %bitcast.74, bf16[512,1024]{1,0:T(8,128)(2,1)S(1)} %copy-done), kind=kOutput, calls=%fused_computation.6 | convolution fusion | flops 1073741824 | bytes 6291456 | tf_op jit(solution)/shard_map/dot_general | solution.py:86
  137.3 6.7 %reshape.42 = f32[2,512,4,256]{1,0,3,2:T(2,128)} reshape(f32[1024,1024]{0,1:T(8,128)} %convolution_bitcast_fusion) | data formatting | bytes 8388608 | tf_op jit(solution)/shard_map/reshape | solution.py:92
  144.0 7.3 %copy.75 = f32[2,4,512,256]{3,2,1,0:T(8,128)} copy(f32[2,4,512,256]{2,0,3,1:T(2,128)} %bitcast.71) | data formatting | bytes 8388608 | tf_op jit(solution)/shard_map/transpose | solution.py:93
  151.3 0.9 copy-done.14
  152.4 1.0 slice.138
  153.4 3.6 %collective-permute-start.4 = (bf16[512,133]{0,1:T(8,128)(2,1)S(1)}, bf16[512,133]{0,1:T(8,128)(2,1)S(1)}, u32[]{:S(2)}, u32[]{:S(2)}) collective-permute-start(bf16[512,133]{0,1:T(8,128)(2,1)S(1)} %slice.138), channel_id=1, source_target_pairs={{8,0},{16,8},{24,16},{9,1},{17,9},{25,17},{10,2},{18,10},{26,18},{... | collective-permute-start | bytes 408584 | tf_op jit(solution)/shard_map/ppermute | solution.py:32
  157.0 4.6 %reduce-precision_reduce_fusion = bf16[512,1024]{1,0:T(8,128)(2,1)} fusion(bf16[512,4,256]{2,0,1:T(8,128)(2,1)} %all_to_all.15, bf16[1024,4,256]{0,2,1:T(8,128)(2,1)} %bitcast.83), kind=kOutput, calls=%fused_computation | convolution fusion | flops 1079508992 | bytes 4194304 | tf_op jit(solution)/shard_map/dot_general | solution.py:103
  161.8 1.1 copy-done.4
  163.0 5.4 %fusion.18 = f32[1,512,262]{1,0,2:T(1,128)S(1)} fusion(f32[512,1,128]{0,1,2:T(1,128)S(1)} %copy.79, f32[1,512,389]{1,2,0:T(8,128)S(1)} %bitcast.73), kind=kOutput, calls=%fused_computation.32 | convolution fusion | flops 206045184 | bytes 1595392 | tf_op jit(solution)/shard_map/conv_general_dilated | solution.py:36
  168.9 1.1 copy.80
  170.0 2.4 %reshape.74 = f32[1536,1,262]{0,2,1:T(8,128)} reshape(f32[3,512,262]{1,0,2:T(4,128)S(1)} %copy.80) | data formatting | bytes 3219456 | tf_op jit(solution)/shard_map/broadcast_in_dim;reshape | solution.py:37
  172.4 2.7 %pad.2 = f32[1536,1,264]{0,2,1:T(8,128)} pad(f32[1536,1,262]{0,2,1:T(8,128)} %reshape.74, f32[]{:T(128)} %constant.11.clone.1), padding=0_0x0_0x0_2 | pad | bytes 3231748 | tf_op jit(solution)/shard_map/broadcast_in_dim;reshape | solution.py:37
  175.1 3.3 %reshape.60 = f32[1536,1,8,33]{0,1,3,2:T(1,128)S(1)} reshape(f32[1536,1,264]{0,2,1:T(8,128)} %pad.2) | data formatting | bytes 3244032 | tf_op jit(solution)/shard_map/conv_general_dilated | solution.py:36
  178.6 0.5 copy-done.20
  179.0 1.5 fusion.1
  180.8 0.3 reshape.64
  181.1 19.7 %reduce-scatter.3.cloned.1.call-done = f32[512,256]{1,0:T(8,128)} async-done(((f32[4096,256]{1,0:T(8,128)}), f32[512,256]{1,0:T(8,128)}) %reduce-scatter.3.cloned.1.call-update) | async-done | bytes 524304 | tf_op jit(solution)/shard_map/reduce_scatter | solution.py:96
  200.8 1.2 convert_element_type.21
  202.0 1.9 collective-permute-start.2
  204.0 1.2 copy.85
  205.1 17.6 %collective-permute-done.2 = bf16[512,256]{1,0:T(8,128)(2,1)S(1)} collective-permute-done((bf16[512,256]{1,0:T(8,128)(2,1)S(1)}, bf16[512,256]{1,0:T(8,128)(2,1)S(1)}, u32[]{:S(2)}, u32[]{:S(2)}) %collective-permute-start.2) | collective-permute-done | bytes 262176 | tf_op jit(solution)/shard_map/ppermute | solution.py:101
  222.7 0.7 copy.104
  (59 shorter events, 2.5 us)
Async XLA Ops:
  7.2 57.0 %copy-start = (bf16[512,1024]{1,0:T(8,128)(2,1)S(1)}, bf16[512,1024]{1,0:T(8,128)(2,1)}, u32[]{:S(2)}) copy-start(bf16[512,1024]{1,0:T(8,128)(2,1)} %param.10) | copy-start | bytes 3145732
  7.2 22.1 %copy-start.2 = (bf16[3,512,256]{2,1,0:T(8,128)(2,1)S(1)}, bf16[3,512,256]{2,1,0:T(8,128)(2,1)}, u32[]{:S(2)}) copy-start(bf16[3,512,256]{2,1,0:T(8,128)(2,1)} %param.6) | copy-start | bytes 2359300
  7.2 56.9 %all-gather.2.cloned.1.call-start = ((), (), s32[]{:S(2)}) async-start(), calls=%async_computation.5 | async-start | bytes 2359296 | tf_op jit(solution)/shard_map/all_gather | solution.py:59
  16.4 12.1 %collective-permute-start.3 = (bf16[128,1024]{0,1:T(8,128)(2,1)S(1)}, bf16[128,1024]{0,1:T(8,128)(2,1)S(1)}, u32[]{:S(2)}, u32[]{:S(2)}) collective-permute-start(bf16[128,1024]{0,1:T(8,128)(2,1)S(1)} %bitcast.80), channel_id=1, source_target_pairs={{0,0},{1,4},{2,8},{3,12},{4,16},{5,20},{6,24},{7,28},{8,1},{9,5},{... | collective-permute-start | bytes 786440 | tf_op jit(solution)/shard_map/ppermute | solution.py:58
  28.5 0.7 copy-start.16
  29.2 123.1 %reduce-scatter.5.cloned.1.call-start = ((), (), s32[]{:S(2)}) async-start(), calls=%async_computation.6 | async-start | bytes 2621440 | tf_op jit(solution)/shard_map/reduce_scatter | solution.py:73
  29.6 9.2 %copy-start.17 = (f32[3,512,7]{1,2,0:T(8,128)S(1)}, f32[3,512,7]{1,2,0:T(8,128)}, u32[]{:S(2)}) copy-start(f32[3,512,7]{1,2,0:T(8,128)} %param.7) | copy-start | bytes 129028
  29.7 9.6 %copy-start.13 = (f32[512,128]{1,0:T(8,128)S(1)}, f32[512,128]{1,0:T(8,128)}, u32[]{:S(2)}) copy-start(f32[512,128]{1,0:T(8,128)} %param.8) | copy-start | bytes 786436
  30.7 16.7 %collective-permute-start = (bf16[3,512,133]{1,2,0:T(8,128)(2,1)}, bf16[3,512,133]{1,2,0:T(8,128)(2,1)S(1)}, u32[]{:S(2)}, u32[]{:S(2)}) collective-permute-start(bf16[3,512,133]{1,2,0:T(8,128)(2,1)} %copy.91), channel_id=1, source_target_pairs={{0,8},{8,16},{16,24},{1,9},{9,17},{17,25},{2,10},{10,18},{18,26},{... | collective-permute-start | bytes 1225736 | tf_op jit(solution)/shard_map/ppermute | solution.py:21
  35.6 16.4 %collective-permute-start.1 = (bf16[3,512,133]{1,2,0:T(8,128)(2,1)S(1)}, bf16[3,512,133]{1,2,0:T(8,128)(2,1)S(1)}, u32[]{:S(2)}, u32[]{:S(2)}) collective-permute-start(bf16[3,512,133]{1,2,0:T(8,128)(2,1)S(1)} %copy.92), channel_id=1, source_target_pairs={{8,0},{16,8},{24,16},{9,1},{17,9},{25,17},{10,2},{18,10},{26,18},{... | collective-permute-start | bytes 1225736 | tf_op jit(solution)/shard_map/ppermute | solution.py:24
  62.9 1.2 copy-start.10
  68.4 1.4 copy-start.11
  68.4 1.4 copy-start.19
  68.4 132.4 %reduce-scatter.3.cloned.1.call-start = ((), (), s32[]{:S(2)}) async-start(), calls=%async_computation.4 | async-start | bytes 4718592 | tf_op jit(solution)/shard_map/reduce_scatter | solution.py:96
  81.6 2.3 %copy-start.7 = (f32[1,528,512]{2,1,0:T(8,128)S(1)}, f32[1,528,512]{2,1,0:T(8,128)}, u32[]{:S(2)}) copy-start(f32[1,528,512]{2,1,0:T(8,128)} %reshape.53) | copy-start | bytes 3244036
  83.9 1.3 copy-start.8
  85.2 23.6 %copy-start.3 = (f32[512,516]{0,1:T(8,128)}, f32[512,516]{0,1:T(8,128)S(1)}, u32[]{:S(2)}) copy-start(f32[512,516]{0,1:T(8,128)S(1)} %slice_bitcast_fusion.2) | copy-start | bytes 3170308
  85.2 2.0 copy-start.12
  85.2 2.1 copy-start.15
  87.3 21.2 %copy-start.18 = (f32[512]{0:T(512)S(1)}, f32[512]{0:T(512)}, u32[]{:S(2)}) copy-start(f32[512]{0:T(512)} %param.9) | copy-start | bytes 6148
  108.7 0.9 copy-start.5
  151.2 0.9 copy-start.14
  153.4 8.3 %collective-permute-start.4 = (bf16[512,133]{0,1:T(8,128)(2,1)S(1)}, bf16[512,133]{0,1:T(8,128)(2,1)S(1)}, u32[]{:S(2)}, u32[]{:S(2)}) collective-permute-start(bf16[512,133]{0,1:T(8,128)(2,1)S(1)} %slice.138), channel_id=1, source_target_pairs={{8,0},{16,8},{24,16},{9,1},{17,9},{25,17},{10,2},{18,10},{26,18},{... | collective-permute-start | bytes 408584 | tf_op jit(solution)/shard_map/ppermute | solution.py:32
  157.0 4.7 %copy-start.6 = (f32[512,389]{0,1:T(8,128)S(1)}, f32[512,389]{0,1:T(8,128)}, u32[]{:S(2)}) copy-start(f32[512,389]{0,1:T(8,128)} %copy-done.5) | copy-start | bytes 2390020
  157.0 4.7 %copy-start.9 = (f32[512,256]{0,1:T(8,128)S(1)}, f32[512,256]{0,1:T(8,128)}, u32[]{:S(2)}) copy-start(f32[512,256]{0,1:T(8,128)} %reduce-scatter.5.cloned.1.call-done) | copy-start | bytes 1572868
  161.6 1.2 copy-start.4
  178.4 0.7 copy-start.20
  200.8 22.6 %copy-start.1 = (bf16[512,1024]{1,0:T(8,128)(2,1)S(1)}, bf16[512,1024]{1,0:T(8,128)(2,1)}, u32[]{:S(2)}) copy-start(bf16[512,1024]{1,0:T(8,128)(2,1)} %param.10) | copy-start | bytes 3145732
  202.0 20.7 %collective-permute-start.2 = (bf16[512,256]{1,0:T(8,128)(2,1)S(1)}, bf16[512,256]{1,0:T(8,128)(2,1)S(1)}, u32[]{:S(2)}, u32[]{:S(2)}) collective-permute-start(bf16[512,256]{1,0:T(8,128)(2,1)S(1)} %convert_element_type.21), channel_id=1, source_target_pairs={{0,0},{1,8},{2,16},{3,24},{4,1},{5,9},{6,17},{7,25},{8,2},{9,10},{... | collective-permute-start | bytes 786440 | tf_op jit(solution)/shard_map/ppermute | solution.py:101
Sparse Core Ops, SparseCore 0:
  29.3 32.7 all-gather.1
  68.5 37.1 reduce-scatter.4
  151.4 49.3 reduce-scatter.2
